TPU v7x, 32 devices: a whole 2x2x4 slice. The times are simulated.
32 devices in a mesh: block: 8 (over y, x, core), tm: 4 (over z).
Axes of the slice: x: 2, y: 2, z: 4, core: 2. Of those that a mesh axis runs over, the one named last changes fastest.
Arguments:
- traces: bfloat16 [2048, 8, 6, 1024], P('block', 'tm')
- valid: int32 [2048, 8, 6], P('block', 'tm'), may hold values from 0 to 1, as said below
- panel_owner: int32 [4], replicated, may hold values from 0 to 7, as said below
- panel_start: int32 [4], replicated, may hold values from 0 to 252, as said below
Outputs:
- xcorr: float32 [16, 2048, 1024], P('tm', 'block')
Inputs may be any that keep to these rules, and one draw needn't show every extreme that they name: Within one block-tm cell (256 channels by 2 windows by 6 segments) at least an eighth of the segments are valid. `panel_owner`: the panels lie on distinct blocks. `panel_start`: multiples of 4.
All inputs are finite; a program needn't handle non-finite values.
Results may differ from a plain program's by a relative error of at most 0.0051.
Values may be sent and summed in bfloat16 or wider, within the bound.
No kernel may reach another device: no remote copies, remote signals or barrier semaphores. Data moves between devices by JAX's collectives and lax.ppermute only.
A program may use at most 128 MiB of HBM per device.

v0:
```python
import math

import jax
import jax.numpy as jnp
from jax import lax
from jax.sharding import PartitionSpec as P

PP = 4
NP = 4


def spread(value, axis, source):
    kept = jnp.where(lax.axis_index(axis) == source, value, 0).astype(value.dtype)
    return lax.psum(kept, axis)


def forward_table(length):
    sample = jnp.arange(length, dtype=jnp.int32)
    bin_index = jnp.arange(length // 2, dtype=jnp.int32)
    angles = (sample[:, None] * bin_index[None, :] % length).astype(jnp.float32) * (
        2.0 * math.pi / length
    )
    return jnp.concatenate([jnp.cos(angles), -jnp.sin(angles)], axis=1).astype(jnp.bfloat16)


def inverse_table(length, factor):
    bin_index = jnp.arange(length // 2, dtype=jnp.int32)
    lag_index = jnp.arange(length, dtype=jnp.int32)
    angles = (bin_index[:, None] * lag_index[None, :] % length).astype(jnp.float32) * (
        2.0 * math.pi / length
    )
    weight = jnp.where(bin_index == 0, 1.0, 2.0).astype(jnp.float32)[:, None] * factor
    return jnp.concatenate([weight * jnp.cos(angles), -weight * jnp.sin(angles)], axis=0)


def whiten(segment_rows, valid_mask, forward):
    spectrum = jnp.dot(segment_rows, forward, preferred_element_type=jnp.float32)
    energy = jnp.mean(spectrum * spectrum, axis=1, keepdims=True)
    return (spectrum * lax.rsqrt(energy + 1e-06) * valid_mask[:, None].astype(jnp.float32)).astype(
        jnp.bfloat16
    )


def spectra_rows(segment_rows, valid_mask, forward):
    return whiten(segment_rows, valid_mask, forward)


def correlate(left, right):
    bins = left.shape[-1] // 2
    left_both = jnp.concatenate([left[..., :bins], left[..., bins:]], axis=1)
    right_both = jnp.concatenate([right[..., :bins], right[..., bins:]], axis=1)
    right_turn = jnp.concatenate([right[..., bins:], -right[..., :bins]], axis=1)
    real_part = jnp.einsum(
        "jmk,imk->jik", left_both, right_both, preferred_element_type=jnp.float32
    )
    imag_part = jnp.einsum(
        "jmk,imk->jik", left_both, right_turn, preferred_element_type=jnp.float32
    )
    return jnp.concatenate([real_part, imag_part], axis=-1)


def fetch_panel(whitened, panel_root, panel_first):
    candidate = lax.dynamic_slice_in_dim(whitened, panel_first, PP, 0)
    return spread(candidate, "block", panel_root)


def on_device(traces, valid, panel_owner, panel_start):
    channels, windows_here, segments, length = traces.shape
    bins = length // 2
    forward = forward_table(length)
    whitened = spectra_rows(
        traces.reshape(channels * windows_here * segments, length),
        valid.reshape(channels * windows_here * segments),
        forward,
    )
    whitened = whitened.reshape(channels, windows_here, segments, 2 * bins)
    pieces = []
    for panel in range(NP):
        pieces.append(fetch_panel(whitened, panel_owner[panel], panel_start[panel]))
    sources = jnp.concatenate(pieces, axis=0)
    groups = lax.axis_size("tm")
    inverse = inverse_table(length, 1.0 / math.sqrt(bins * windows_here * segments * groups))
    source_count = sources.shape[0]
    own_rows = whitened.reshape(channels, windows_here * segments, 2 * bins)
    source_rows = sources.reshape(source_count, windows_here * segments, 2 * bins)
    stacked = lax.psum_scatter(
        correlate(source_rows, own_rows), "tm", scatter_dimension=0, tiled=True
    )
    return jnp.dot(stacked, inverse, precision=lax.Precision.HIGHEST)


def solution(mesh):
    in_specs = (P("block", "tm", None, None), P("block", "tm", None), P(), P())
    out_specs = P("tm", "block", None)
    return jax.shard_map(
        on_device, mesh=mesh, in_specs=in_specs, out_specs=out_specs, check_vma=False
    )
```

profile of v0, /device:TPU:0, one launch (start us, length us, event | category | flops | bytes accessed | tf_op | source)
XLA Modules:
  0.0 503.0 jit_solution(8743341185815078538)
XLA Ops:
  6.5 0.0 all-reduce.3.cloned.1.call-start
  6.5 1.5 fusion.26
  13.2 8.5 %negate_convert_fusion = (bf16[1024,512]{1,0:T(8,128)(2,1)S(1)}, bf16[1024,512]{1,0:T(8,128)(2,1)S(1)}) fusion(), kind=kLoop, calls=%fused_computation.30 | loop fusion | flops 8912896 | bytes 2097152 | tf_op jit(solution)/shard_map/convert.1
  21.7 8.9 %copy.5 = bf16[256,2,6,1024]{3,2,1,0:T(8,128)(2,1)} copy(bf16[256,2,6,1024]{3,1,2,0:T(2,128)(2,1)} %param.4) | data formatting | bytes 12582912 | tf_op args[0]
  30.7 11.0 %reshape.36 = bf16[3072,1024]{1,0:T(8,128)(2,1)} reshape(bf16[256,2,6,1024]{3,2,1,0:T(8,128)(2,1)} %copy.5) | data formatting | bytes 12582912 | tf_op jit(solution)/shard_map/reshape | solution.py:72
  41.7 0.0 copy-start
  41.7 12.5 %multiply_reduce_fusion = (f32[3072]{0:T(1024)S(1)}, f32[1024,3072]{1,0:T(8,128)}) fusion(bf16[3072,1024]{1,0:T(8,128)(2,1)} %reshape.36, bf16[1024,512]{1,0:T(8,128)(2,1)S(1)} %get-tuple-element.30, bf16[1024,512]{1,0:T(8,128)(2,1)S(1)} %get-tuple-element.31), kind=kOutput, calls=%fused_computation.2 | convolution fusion | flops 6452933632 | bytes 20983808 | tf_op jit(solution)/shard_map/dot_general | solution.py:37
  54.2 0.0 copy-done
  54.2 0.2 copy.6
  54.4 0.3 convert_element_type.35
  54.7 9.0 %fusion = bf16[3072,1024]{0,1:T(8,128)(2,1)} fusion(f32[1024,3072]{1,0:T(8,128)} %get-tuple-element.29, f32[3072]{0:T(1024)S(1)} %convert_element_type.35, f32[3072]{0:T(1024)S(1)} %add_rsqrt_fusion), kind=kLoop, calls=%fused_computation.3 | loop fusion | flops 9437184 | bytes 18898944 | tf_op jit(solution)/shard_map/convert_element_type | solution.py:39
  63.7 8.6 %copy.7 = bf16[3072,1024]{1,0:T(8,128)(2,1)} copy(bf16[3072,1024]{0,1:T(8,128)(2,1)} %fusion) | data formatting | bytes 12582912 | tf_op jit(solution)/shard_map/convert_element_type | solution.py:39
  72.3 0.0 copy-start.1
  72.3 11.0 %reshape.37 = bf16[256,2,6,1024]{3,2,1,0:T(8,128)(2,1)} reshape(bf16[3072,1024]{1,0:T(8,128)(2,1)} %copy.7) | data formatting | bytes 12582912 | tf_op jit(solution)/shard_map/reshape | solution.py:76
  83.3 0.0 copy-done.1
  83.3 0.7 fusion.25
  89.0 1.9 dynamic-slice_select_fusion.3
  90.9 0.0 all-reduce.3.cloned.1.call-update
  91.0 0.2 reduce-scatter.2.cloned.1.call-start
  91.2 10.6 %reshape_reshape.3 = bf16[256,12,1024]{2,1,0:T(8,128)(2,1)} reshape(bf16[3072,1024]{1,0:T(8,128)(2,1)} %copy.7) | data formatting | bytes 12582912 | tf_op jit(solution)/shard_map/reshape;reshape | solution.py:84
  101.8 3.9 fusion.23
  105.8 7.8 %pad_maximum_fusion.1 = (bf16[256,24,512]{2,1,0:T(8,128)(2,1)}, bf16[256,24,512]{2,1,0:T(8,128)(2,1)}) fusion(bf16[256,12,512]{2,1,0:T(8,128)(2,1)S(1)} %get-tuple-element.11, bf16[256,12,512]{2,1,0:T(8,128)(2,1)S(1)} %get-tuple-element.9, bf16[256,12,512]{2,1,0:T(8,128)(2,1)S(1)} %get-tuple-element.10), kind=kLoop, calls=%fused_computation.4 | loop fusion | flops 25165824 | bytes 22020096 | tf_op jit(solution)/shard_map/concatenate | solution.py:51
  113.5 9.6 %copy.10 = bf16[256,24,512]{0,1,2:T(8,128)(2,1)} copy(bf16[256,24,512]{2,1,0:T(8,128)(2,1)} %get-tuple-element.16) | data formatting | bytes 12582912 | tf_op jit(solution)/shard_map/concatenate | solution.py:51
  123.2 9.6 %copy.13 = bf16[256,24,512]{0,1,2:T(8,128)(2,1)} copy(bf16[256,24,512]{2,1,0:T(8,128)(2,1)} %get-tuple-element.17) | data formatting | bytes 12582912 | tf_op jit(solution)/shard_map/concatenate | solution.py:52
  132.7 16.0 %all-reduce.3.cloned.1.call-done = (bf16[4,2,6,1024]{3,2,1,0:T(8,128)(2,1)}, bf16[4,2,6,1024]{3,2,1,0:T(8,128)(2,1)}, bf16[4,2,6,1024]{3,2,1,0:T(8,128)(2,1)}, bf16[4,2,6,1024]{3,2,1,0:T(8,128)(2,1)}) async-done(((bf16[4,2,6,1024]{3,2,1,0:T(8,128)(2,1)}, bf16[4,2,6,1024]{3,2,1,0:T(8,128)(2,1)}, bf16[4,2,6,1024]{3,2,1,0:T(8,128)(2,1)}, bf16[4,2,6,1024]{3,2,1,0:T(8,128)(2,1)}), ...) | async-done | bytes 393232 | tf_op jit(solution)/shard_map/psum | solution.py:14
  148.7 1.2 pad_maximum_fusion.3
  150.0 0.2 copy.9
  150.3 2.1 copy.11
  152.4 7.2 %fusion.27 = f32[512,256,16]{1,2,0:T(8,128)} fusion(bf16[256,24,512]{0,1,2:T(8,128)(2,1)} %copy.10, bf16[16,24,512]{1,0,2:T(8,128)(2,1)S(1)} %copy.11), kind=kOutput, calls=%fused_computation.53 | convolution fusion | flops 100663296 | bytes 15073280 | tf_op jit(solution)/shard_map/jmk,imk->jik/dot_general | solution.py:53
  159.7 10.0 %copy.12 = f32[512,256,16]{0,1,2:T(8,128)} copy(f32[512,256,16]{1,2,0:T(8,128)} %fusion.27) | data formatting | bytes 16777216 | tf_op jit(solution)/shard_map/jmk,imk->jik/dot_general | solution.py:53
  169.6 7.2 %fusion.28 = f32[512,256,16]{1,2,0:T(8,128)} fusion(bf16[256,24,512]{0,1,2:T(8,128)(2,1)} %copy.13, bf16[16,24,512]{1,0,2:T(8,128)(2,1)S(1)} %copy.11), kind=kOutput, calls=%fused_computation.54 | convolution fusion | flops 100663296 | bytes 15073280 | tf_op jit(solution)/shard_map/jmk,imk->jik/dot_general | solution.py:56
  176.8 10.0 %copy.14 = f32[512,256,16]{0,1,2:T(8,128)} copy(f32[512,256,16]{1,2,0:T(8,128)} %fusion.28) | data formatting | bytes 16777216 | tf_op jit(solution)/shard_map/jmk,imk->jik/dot_general | solution.py:56
  186.8 11.8 %pad_maximum_fusion = f32[16,256,1024]{2,1,0:T(8,128)} fusion(f32[16,256,512]{2,1,0:T(8,128)} %bitcast.23, f32[16,256,512]{2,1,0:T(8,128)} %bitcast.22), kind=kLoop, calls=%fused_computation | loop fusion | flops 4194304 | bytes 33554432 | tf_op jit(solution)/shard_map/concatenate | solution.py:59
  198.6 0.0 reduce-scatter.2.cloned.1.call-update
  198.6 9.2 %sine_multiply_fusion = (f32[512,1024]{1,0:T(8,128)S(1)}, f32[512,1024]{1,0:T(8,128)}) fusion(f32[512]{0:T(512)S(1)} %fusion.20, f32[512]{0:T(512)S(1)} %select_multiply_fusion), kind=kLoop, calls=%fused_computation.26 | loop fusion | flops 8388608 | bytes 4198400 | tf_op jit(solution)/shard_map/mul | solution.py:33
  207.8 270.6 %reduce-scatter.2.cloned.1.call-done = f32[4,256,1024]{2,1,0:T(8,128)} async-done(((f32[16,256,1024]{2,1,0:T(8,128)}), f32[4,256,1024]{2,1,0:T(8,128)}) %reduce-scatter.2.cloned.1.call-update) | async-done | bytes 4194320 | tf_op jit(solution)/shard_map/reduce_scatter | solution.py:86
  478.4 17.8 %fusion.1 = f32[4,256,1024]{2,1,0:T(8,128)} fusion(f32[4,256,1024]{2,1,0:T(8,128)} %reduce-scatter.2.cloned.1.call-done, f32[512,1024]{1,0:T(8,128)S(1)} %get-tuple-element.32, f32[512,1024]{1,0:T(8,128)} %get-tuple-element.33), kind=kOutput, calls=%fused_computation.7 | convolution fusion | flops 12885950464 | bytes 12582912 | tf_op jit(solution)/shard_map/dot_general | solution.py:89
  (6 shorter events, 0.1 us)
Async XLA Ops:
  6.5 142.2 %all-reduce.3.cloned.1.call-start = ((), (), s32[]{:S(2)}) async-start(), calls=%async_computation.2 | async-start | bytes 1048576 | tf_op jit(solution)/shard_map/psum | solution.py:14
  41.7 12.5 %copy-start = (s32[256,2,6]{0,1,2:T(2,128)S(1)}, s32[256,2,6]{0,1,2:T(2,128)}, u32[]{:S(2)}) copy-start(s32[256,2,6]{0,1,2:T(2,128)} %param.5) | copy-start | bytes 36868
  72.3 11.0 %copy-start.1 = (s32[4]{0:T(128)S(1)}, s32[4]{0:T(128)}, u32[]{:S(2)}) copy-start(s32[4]{0:T(128)} %param.6) | copy-start | bytes 52
  91.0 387.4 %reduce-scatter.2.cloned.1.call-start = ((), (), s32[]{:S(2)}) async-start(), calls=%async_computation.1 | async-start | bytes 20971520 | tf_op jit(solution)/shard_map/reduce_scatter | solution.py:86
Sparse Core Ops, SparseCore 0:
  91.1 57.6 all-reduce.2
  198.7 279.6 reduce-scatter.1
where the time goes:
time: 505 us; the launch traced here: 503 us
  waiting for transfers between devices  287 us (57%)
  local copies, waits for them, and re-layouts  94.4 us (19%)
  other arithmetic  53.4 us (11%)
  matrix products  44.7 us (9%)
  between operations  23.7 us (5%)
    reduce_scatter x1, waiting for transfers between devices, on_device(): lax.psum_scatter(correlate(source_rows, own_rows), 'tm', scatter_dimensio...  271 us
    dot_general x1, matrix products, on_device(): return jnp.dot(stacked, inverse, precision=lax.Precision.HIGHEST)  17.8 us
    psum x1, waiting for transfers between devices, spread(): return lax.psum(kept, axis)  16 us
    dot_general x1, matrix products, whiten(): jnp.dot(segment_rows, forward, preferred_element_type=jnp.float32)  12.5 us
    concatenate x1, other arithmetic, correlate(): return jnp.concatenate([real_part, imag_part], axis=-1)  11.8 us
    reshape x1, local copies, waits for them, and re-layouts, on_device(): traces.reshape(channels * windows_here * segments, length)  11 us
    reshape x1, local copies, waits for them, and re-layouts, on_device(): whitened = whitened.reshape(channels, windows_here, segments, 2 * bins)  11 us
    another operation x1, local copies, waits for them, and re-layouts, on_device(): own_rows = whitened.reshape(channels, windows_here * segments, 2 * bins)  10.6 us
  transfers between devices with their start and end apart: 2, of which 2 were waited for; matrix products, arithmetic and copies ran while one was open for 10% of the time, Pallas kernels for 0%

commit v1 on v0

--- a/solution.py
+++ b/solution.py
@@ -89,9 +89,60 @@
     return jnp.dot(stacked, inverse, precision=lax.Precision.HIGHEST)
 
 
+def edge_first(values, groups):
+    return lax.ppermute(values, "tm", [(0, 1), (groups - 1, groups - 2)])
+
+
+def on_line(traces, valid, panel_owner, panel_start):
+    channels, windows_here, segments, length = traces.shape
+    bins = length // 2
+    groups = lax.axis_size("tm")
+    place = lax.axis_index("tm")
+    forward = forward_table(length)
+    whitened = spectra_rows(
+        traces.reshape(channels * windows_here * segments, length),
+        valid.reshape(channels * windows_here * segments),
+        forward,
+    ).reshape(channels, windows_here * segments, 2 * bins)
+    pieces = []
+    for panel in range(NP):
+        pieces.append(fetch_panel(whitened, panel_owner[panel], panel_start[panel]))
+    sources = jnp.concatenate(pieces, axis=0)
+    source_count = sources.shape[0]
+    per_group = source_count // groups
+    half = source_count // 2
+    edge_sources = edge_first(sources, groups)
+    inverse = inverse_table(length, 1.0 / math.sqrt(bins * windows_here * segments * groups))
+    first_half = place < groups // 2
+    chunks = 4
+    width = channels // chunks
+    outs = []
+    for chunk in range(chunks):
+        own = whitened[chunk * width:(chunk + 1) * width]
+        edge_rows = edge_first(own, groups)
+        partial = correlate(sources, own) + correlate(edge_sources, edge_rows)
+        low = partial[:half]
+        high = partial[half:]
+        to_right = lax.ppermute(high, "tm", [(1, 2)])
+        to_left = lax.ppermute(low, "tm", [(2, 1)])
+        total = jnp.where(first_half, low + to_left, high + to_right)
+        lower = total[:per_group]
+        upper = total[per_group:]
+        back_left = lax.ppermute(lower, "tm", [(1, 0)])
+        back_right = lax.ppermute(upper, "tm", [(2, 3)])
+        final = jnp.where(
+            place == 0,
+            back_left,
+            jnp.where(place == groups - 1, back_right, jnp.where(first_half, upper, lower)),
+        )
+        outs.append(jnp.dot(final, inverse, precision=lax.Precision.HIGHEST))
+    return jnp.concatenate(outs, axis=1)
+
+
 def solution(mesh):
     in_specs = (P("block", "tm", None, None), P("block", "tm", None), P(), P())
     out_specs = P("tm", "block", None)
+    body = on_line if mesh.shape["tm"] == 4 else on_device
     return jax.shard_map(
-        on_device, mesh=mesh, in_specs=in_specs, out_specs=out_specs, check_vma=False
+        body, mesh=mesh, in_specs=in_specs, out_specs=out_specs, check_vma=False
     )

time: 505 us -> 645 us (1.28)
  the two profiles are of different devices: /device:TPU:0 before, /device:TPU:16 now
where the time goes in v1:
time: 645 us; the launch traced here: 633 us
  local copies, waits for them, and re-layouts  333 us (52%)
  other arithmetic  123 us (19%)
  matrix products  91.2 us (14%)
  starting transfers between devices  52.4 us (8%)
  between operations  24.2 us (4%)
  waiting for transfers between devices  9.7 us (2%)
    unnamed x115, local copies, waits for them, and re-layouts  102 us
    slice x13, local copies, waits for them, and re-layouts, on_line(): own = whitened[chunk * width:(chunk + 1) * width]  39.7 us
    dot_general x8, matrix products, correlate(): jnp.einsum('jmk,imk->jik', left_both, right_both, preferred_element_type=...  33.8 us
    slice x8, local copies, waits for them, and re-layouts, on_line(): low = partial[:half]  32.1 us
    dot_general x8, matrix products, correlate(): jnp.einsum('jmk,imk->jik', left_both, right_turn, preferred_element_type=...  27.5 us
    select_n x4, other arithmetic, on_line(): total = jnp.where(first_half, low + to_left, high + to_right)  26.7 us
    ppermute x4, starting transfers between devices, on_line(): to_left = lax.ppermute(low, 'tm', [(2, 1)])  25.1 us
    neg x8, other arithmetic, correlate(): -right[..., :bins]  24 us
  transfers between devices with their start and end apart: 22, of which 1 were waited for; matrix products, arithmetic and copies ran while one was open for 72% of the time, Pallas kernels for 0%

profile of v1, /device:TPU:16, one launch (start us, length us, event | category | flops | bytes accessed | tf_op | source)
XLA Modules:
  0.0 633.4 jit_solution(625792259991723640)
XLA Ops:
  6.5 8.5 %negate_convert_fusion = (bf16[1024,512]{1,0:T(8,128)(2,1)S(1)}, bf16[1024,512]{1,0:T(8,128)(2,1)S(1)}) fusion(), kind=kLoop, calls=%fused_computation.127 | loop fusion | flops 8912896 | bytes 2097152 | tf_op jit(solution)/shard_map/convert.1
  15.1 9.1 %copy.135 = bf16[256,2,6,1024]{3,2,1,0:T(8,128)(2,1)} copy(bf16[256,2,6,1024]{3,1,2,0:T(2,128)(2,1)} %param.4) | data formatting | bytes 12582912 | tf_op args[0]
  24.2 11.0 %reshape.37 = bf16[3072,1024]{1,0:T(8,128)(2,1)} reshape(bf16[256,2,6,1024]{3,2,1,0:T(8,128)(2,1)} %copy.135) | data formatting | bytes 12582912 | tf_op jit(solution)/shard_map/reshape | solution.py:103
  35.2 12.5 %multiply_reduce_fusion = (f32[3072]{0:T(1024)S(1)}, f32[1024,3072]{1,0:T(8,128)}) fusion(bf16[3072,1024]{1,0:T(8,128)(2,1)} %reshape.37, bf16[1024,512]{1,0:T(8,128)(2,1)S(1)} %get-tuple-element.63, bf16[1024,512]{1,0:T(8,128)(2,1)S(1)} %get-tuple-element.64), kind=kOutput, calls=%fused_computation.1 | convolution fusion | flops 6452933632 | bytes 20983808 | tf_op jit(solution)/shard_map/dot_general | solution.py:37
  48.2 6.4 %fusion = bf16[3072,1024]{0,1:T(8,128)(2,1)S(1)} fusion(f32[1024,3072]{1,0:T(8,128)} %get-tuple-element.62, f32[3072]{0:T(1024)S(1)} %convert_element_type.35, f32[3072]{0:T(1024)S(1)} %add_rsqrt_fusion), kind=kLoop, calls=%fused_computation.6 | loop fusion | flops 9437184 | bytes 18898944 | tf_op jit(solution)/shard_map/convert_element_type | solution.py:39
  106.6 8.7 %copy.140 = bf16[3072,1024]{1,0:T(8,128)(2,1)} copy(bf16[3072,1024]{0,1:T(8,128)(2,1)} %copy-done.4) | data formatting | bytes 12582912 | tf_op jit(solution)/shard_map/convert_element_type | solution.py:39
  115.3 10.6 %reshape.38 = bf16[256,12,1024]{2,1,0:T(8,128)(2,1)} reshape(bf16[3072,1024]{1,0:T(8,128)(2,1)} %copy.140) | data formatting | bytes 12582912 | tf_op jit(solution)/shard_map/reshape | solution.py:106
  141.5 4.3 copy.206
  147.8 4.3 copy.207
  152.1 5.2 copy.210
  160.6 5.1 copy.211
  165.7 5.1 copy.214
  174.2 5.1 copy.215
  179.3 5.1 copy.218
  184.4 14.9 %copy.219 = bf16[64,12,512]{0,1,2:T(8,128)(2,1)} copy(bf16[64,12,512]{2,1,0:T(8,128)(2,1)S(1)} %get-tuple-element.39) | data formatting | bytes 1572864
  202.6 9.5 %sine_multiply_fusion = (f32[512,1024]{1,0:T(8,128)}, f32[512,1024]{1,0:T(8,128)}) fusion(f32[512]{0:T(512)S(1)} %fusion.137, f32[512]{0:T(512)S(1)} %select_multiply_fusion), kind=kLoop, calls=%fused_computation.122 | loop fusion | flops 8388608 | bytes 4198400 | tf_op jit(solution)/shard_map/mul | solution.py:33
  276.1 5.6 fusion.104
  286.7 3.9 maximum_add_fusion
  290.7 4.2 fusion.159
  311.7 3.9 copy.212
  321.7 5.6 fusion.92
  332.4 3.9 maximum_add_fusion.1
  336.3 4.1 fusion.160
  345.9 7.2 %collective-permute-start.7 = (f32[8,64,1024]{2,1,0:T(8,128)}, f32[8,64,1024]{2,1,0:T(8,128)}, u32[]{:S(2)}, u32[]{:S(2)}) collective-permute-start(f32[8,64,1024]{2,1,0:T(8,128)} %copy.167), channel_id=1, source_target_pairs={{2,1},{6,5},{10,9},{14,13},{18,17},{22,21},{26,25},{30,29}} | collective-permute-start | bytes 6291464 | tf_op jit(solution)/shard_map/ppermute | solution.py:127
  370.5 5.6 fusion.80
  381.1 3.9 maximum_add_fusion.2
  385.1 4.2 fusion.161
  394.9 7.1 %collective-permute-start.12 = (f32[8,64,1024]{2,1,0:T(8,128)}, f32[8,64,1024]{2,1,0:T(8,128)}, u32[]{:S(2)}, u32[]{:S(2)}) collective-permute-start(f32[8,64,1024]{2,1,0:T(8,128)} %copy.182), channel_id=1, source_target_pairs={{2,1},{6,5},{10,9},{14,13},{18,17},{22,21},{26,25},{30,29}} | collective-permute-start | bytes 6291464 | tf_op jit(solution)/shard_map/ppermute | solution.py:127
  404.5 4.2 copy.220
  424.8 6.3 %maximum_add_fusion.3 = f32[16,64,1024]{1,0,2:T(8,128)S(1)} fusion(f32[16,64,512]{1,0,2:T(8,128)} %fusion.71, f32[16,64,512]{1,0,2:T(8,128)} %fusion.74, f32[16,64,512]{1,0,2:T(8,128)} %fusion.65, f32[16,64,512]{1,0,2:T(8,128)} %fusion.68), kind=kLoop, calls=%fused_computation.5 | loop fusion | flops 3145728 | bytes 12582912 | tf_op jit(solution)/shard_map/add | solution.py:123
  431.1 4.1 fusion.162
  449.7 7.1 %collective-permute-start.17 = (f32[8,64,1024]{2,1,0:T(8,128)}, f32[8,64,1024]{2,1,0:T(8,128)}, u32[]{:S(2)}, u32[]{:S(2)}) collective-permute-start(f32[8,64,1024]{2,1,0:T(8,128)} %copy.197), channel_id=1, source_target_pairs={{2,1},{6,5},{10,9},{14,13},{18,17},{22,21},{26,25},{30,29}} | collective-permute-start | bytes 6291464 | tf_op jit(solution)/shard_map/ppermute | solution.py:127
  460.7 6.7 %add_select_fusion.3 = f32[8,64,1024]{1,0,2:T(8,128)S(1)} fusion(f32[8,64,1024]{1,0,2:T(8,128)} %copy.155, f32[8,64,1024]{1,0,2:T(8,128)} %copy.153, pred[]{:T(512)S(6)} %lt.31, f32[16,64,1024]{1,0,2:T(8,128)} %copy-done), kind=kLoop, calls=%fused_computation.12 | loop fusion | flops 1572864 | bytes 10485761 | tf_op jit(solution)/shard_map/jit(_where)/select_n | solution.py:128
  474.9 3.9 copy.168
  481.1 4.0 copy.170
  485.1 6.6 %add_select_fusion.2 = f32[8,64,1024]{1,0,2:T(8,128)S(1)} fusion(f32[8,64,1024]{1,0,2:T(8,128)} %copy.170, f32[8,64,1024]{1,0,2:T(8,128)} %copy.168, pred[]{:T(512)S(6)} %lt.31, f32[16,64,1024]{1,0,2:T(8,128)} %copy-done.1), kind=kLoop, calls=%fused_computation.11 | loop fusion | flops 1572864 | bytes 10485761 | tf_op jit(solution)/shard_map/jit(_where)/select_n | solution.py:128
  500.4 3.9 copy.183
  510.4 6.7 %add_select_fusion.1 = f32[8,64,1024]{1,0,2:T(8,128)S(1)} fusion(f32[8,64,1024]{1,0,2:T(8,128)} %copy.185, f32[8,64,1024]{1,0,2:T(8,128)} %copy.183, pred[]{:T(512)S(6)} %lt.31, f32[16,64,1024]{1,0,2:T(8,128)} %copy-done.2), kind=kLoop, calls=%fused_computation.10 | loop fusion | flops 1572864 | bytes 10485761 | tf_op jit(solution)/shard_map/jit(_where)/select_n | solution.py:128
  524.1 3.9 copy.198
  528.1 9.6 %collective-permute-done.18 = f32[8,64,1024]{2,1,0:T(8,128)} collective-permute-done((f32[8,64,1024]{2,1,0:T(8,128)}, f32[8,64,1024]{2,1,0:T(8,128)}, u32[]{:S(2)}, u32[]{:S(2)}) %collective-permute-start.18) | collective-permute-done | bytes 2097184 | tf_op jit(solution)/shard_map/ppermute | solution.py:126
  540.0 3.9 copy.200
  543.8 6.6 %add_select_fusion = f32[8,64,1024]{1,0,2:T(8,128)S(1)} fusion(f32[8,64,1024]{1,0,2:T(8,128)} %copy.200, f32[8,64,1024]{1,0,2:T(8,128)} %copy.198, pred[]{:T(512)S(6)} %lt.31, f32[16,64,1024]{1,0,2:T(8,128)} %copy-done.3), kind=kLoop, calls=%fused_computation.9 | loop fusion | flops 1572864 | bytes 10485761 | tf_op jit(solution)/shard_map/jit(_where)/select_n | solution.py:128
  569.2 4.5 select_select_fusion.3
  585.2 4.5 select_select_fusion.2
  589.7 4.8 fusion.127
  602.8 4.5 select_select_fusion.1
  607.3 4.9 fusion.125
  615.1 4.5 select_select_fusion
  (243 shorter events, 318.8 us)
Async XLA Ops:
  6.5 205.6 %all-reduce.3.cloned.1.call-start = ((), (), s32[]{:S(2)}) async-start(), calls=%async_computation | async-start | bytes 1048576 | tf_op jit(solution)/shard_map/psum | solution.py:14
  35.2 12.5 %copy-start.46 = (s32[256,2,6]{0,1,2:T(2,128)S(1)}, s32[256,2,6]{0,1,2:T(2,128)}, u32[]{:S(2)}) copy-start(s32[256,2,6]{0,1,2:T(2,128)} %param.5) | copy-start | bytes 36868
  54.6 4.7 copy-start.4
  66.5 197.3 %collective-permute-start = (bf16[64,12,1024]{2,0,1:T(8,128)(2,1)}, bf16[64,12,1024]{2,0,1:T(8,128)(2,1)}, u32[]{:S(2)}, u32[]{:S(2)}) collective-permute-start(bf16[64,12,1024]{2,0,1:T(8,128)(2,1)} %copy.147), channel_id=1, source_target_pairs={{0,1},{3,2},{4,5},{7,6},{8,9},{11,10},{12,13},{15,14},{16,17},{19,... | collective-permute-start | bytes 4718600 | tf_op jit(solution)/shard_map/ppermute | solution.py:93
  77.6 231.7 %collective-permute-start.6 = (bf16[64,12,1024]{2,0,1:T(8,128)(2,1)}, bf16[64,12,1024]{2,0,1:T(8,128)(2,1)}, u32[]{:S(2)}, u32[]{:S(2)}) collective-permute-start(bf16[64,12,1024]{2,0,1:T(8,128)(2,1)} %copy.164), channel_id=1, source_target_pairs={{0,1},{3,2},{4,5},{7,6},{8,9},{11,10},{12,13},{15,14},{16,17},{19,... | collective-permute-start | bytes 4718600 | tf_op jit(solution)/shard_map/ppermute | solution.py:93
  88.7 268.2 %collective-permute-start.11 = (bf16[64,12,1024]{2,0,1:T(8,128)(2,1)}, bf16[64,12,1024]{2,0,1:T(8,128)(2,1)}, u32[]{:S(2)}, u32[]{:S(2)}) collective-permute-start(bf16[64,12,1024]{2,0,1:T(8,128)(2,1)} %copy.179), channel_id=1, source_target_pairs={{0,1},{3,2},{4,5},{7,6},{8,9},{11,10},{12,13},{15,14},{16,17},{19,... | collective-permute-start | bytes 4718600 | tf_op jit(solution)/shard_map/ppermute | solution.py:93
  96.2 4.9 copy-start.47
  99.8 295.1 %collective-permute-start.16 = (bf16[64,12,1024]{2,0,1:T(8,128)(2,1)}, bf16[64,12,1024]{2,0,1:T(8,128)(2,1)}, u32[]{:S(2)}, u32[]{:S(2)}) collective-permute-start(bf16[64,12,1024]{2,0,1:T(8,128)(2,1)} %copy.194), channel_id=1, source_target_pairs={{0,1},{3,2},{4,5},{7,6},{8,9},{11,10},{12,13},{15,14},{16,17},{19,... | collective-permute-start | bytes 4718600 | tf_op jit(solution)/shard_map/ppermute | solution.py:93
  115.3 10.6 %copy-start.48 = (s32[4]{0:T(128)S(1)}, s32[4]{0:T(128)}, u32[]{:S(2)}) copy-start(s32[4]{0:T(128)} %param.6) | copy-start | bytes 52
  216.3 38.2 %collective-permute-start.1 = (bf16[16,12,1024]{2,0,1:T(8,128)(2,1)S(1)}, bf16[16,12,1024]{2,0,1:T(8,128)(2,1)S(1)}, u32[]{:S(2)}, u32[]{:S(2)}) collective-permute-start(bf16[16,12,1024]{2,0,1:T(8,128)(2,1)S(1)} %pad_maximum_fusion.3), channel_id=1, source_target_pairs={{0,1},{3,2},{4,5},{7,6},{8,9},{11,10},{12,13},{15,14},{16,17},{19,... | collective-permute-start | bytes 1179656 | tf_op jit(solution)/shard_map/ppermute | solution.py:93
  223.6 3.5 copy-start.25
  276.1 5.6 copy-start.18
  276.1 5.6 copy-start.40
  281.8 3.5 copy-start.34
  281.8 5.0 copy-start.35
  290.7 6.0 copy-start
  300.5 144.1 %collective-permute-start.2 = (f32[8,64,1024]{2,1,0:T(8,128)}, f32[8,64,1024]{2,1,0:T(8,128)}, u32[]{:S(2)}, u32[]{:S(2)}) collective-permute-start(f32[8,64,1024]{2,1,0:T(8,128)} %copy.152), channel_id=1, source_target_pairs={{2,1},{6,5},{10,9},{14,13},{18,17},{22,21},{26,25},{30,29}} | collective-permute-start | bytes 6291464 | tf_op jit(solution)/shard_map/ppermute | solution.py:127
  308.0 141.7 %collective-permute-start.3 = (f32[8,64,1024]{2,1,0:T(8,128)}, f32[8,64,1024]{2,1,0:T(8,128)}, u32[]{:S(2)}, u32[]{:S(2)}) collective-permute-start(f32[8,64,1024]{2,1,0:T(8,128)} %copy.154), channel_id=1, source_target_pairs={{1,2},{5,6},{9,10},{13,14},{17,18},{21,22},{25,26},{29,30}} | collective-permute-start | bytes 6291464 | tf_op jit(solution)/shard_map/ppermute | solution.py:126
  321.7 5.6 copy-start.19
  321.7 5.6 copy-start.41
  327.4 5.0 copy-start.33
  336.3 5.8 copy-start.1
  345.9 127.6 %collective-permute-start.7 = (f32[8,64,1024]{2,1,0:T(8,128)}, f32[8,64,1024]{2,1,0:T(8,128)}, u32[]{:S(2)}, u32[]{:S(2)}) collective-permute-start(f32[8,64,1024]{2,1,0:T(8,128)} %copy.167), channel_id=1, source_target_pairs={{2,1},{6,5},{10,9},{14,13},{18,17},{22,21},{26,25},{30,29}} | collective-permute-start | bytes 6291464 | tf_op jit(solution)/shard_map/ppermute | solution.py:127
  356.9 121.9 %collective-permute-start.8 = (f32[8,64,1024]{2,1,0:T(8,128)}, f32[8,64,1024]{2,1,0:T(8,128)}, u32[]{:S(2)}, u32[]{:S(2)}) collective-permute-start(f32[8,64,1024]{2,1,0:T(8,128)} %copy.169), channel_id=1, source_target_pairs={{1,2},{5,6},{9,10},{13,14},{17,18},{21,22},{25,26},{29,30}} | collective-permute-start | bytes 6291464 | tf_op jit(solution)/shard_map/ppermute | solution.py:126
  370.5 5.6 copy-start.20
  370.5 5.6 copy-start.42
  376.1 5.0 copy-start.31
  385.0 6.0 copy-start.2
  394.9 103.8 %collective-permute-start.12 = (f32[8,64,1024]{2,1,0:T(8,128)}, f32[8,64,1024]{2,1,0:T(8,128)}, u32[]{:S(2)}, u32[]{:S(2)}) collective-permute-start(f32[8,64,1024]{2,1,0:T(8,128)} %copy.182), channel_id=1, source_target_pairs={{2,1},{6,5},{10,9},{14,13},{18,17},{22,21},{26,25},{30,29}} | collective-permute-start | bytes 6291464 | tf_op jit(solution)/shard_map/ppermute | solution.py:127
  431.1 5.8 copy-start.3
  444.6 59.7 %collective-permute-start.13 = (f32[8,64,1024]{2,1,0:T(8,128)}, f32[8,64,1024]{2,1,0:T(8,128)}, u32[]{:S(2)}, u32[]{:S(2)}) collective-permute-start(f32[8,64,1024]{2,1,0:T(8,128)} %copy.184), channel_id=1, source_target_pairs={{1,2},{5,6},{9,10},{13,14},{17,18},{21,22},{25,26},{29,30}} | collective-permute-start | bytes 6291464 | tf_op jit(solution)/shard_map/ppermute | solution.py:126
  449.7 72.8 %collective-permute-start.17 = (f32[8,64,1024]{2,1,0:T(8,128)}, f32[8,64,1024]{2,1,0:T(8,128)}, u32[]{:S(2)}, u32[]{:S(2)}) collective-permute-start(f32[8,64,1024]{2,1,0:T(8,128)} %copy.197), channel_id=1, source_target_pairs={{2,1},{6,5},{10,9},{14,13},{18,17},{22,21},{26,25},{30,29}} | collective-permute-start | bytes 6291464 | tf_op jit(solution)/shard_map/ppermute | solution.py:127
  473.6 64.1 %collective-permute-start.18 = (f32[8,64,1024]{2,1,0:T(8,128)}, f32[8,64,1024]{2,1,0:T(8,128)}, u32[]{:S(2)}, u32[]{:S(2)}) collective-permute-start(f32[8,64,1024]{2,1,0:T(8,128)} %copy.199), channel_id=1, source_target_pairs={{1,2},{5,6},{9,10},{13,14},{17,18},{21,22},{25,26},{29,30}} | collective-permute-start | bytes 6291464 | tf_op jit(solution)/shard_map/ppermute | solution.py:126
  478.8 81.1 %collective-permute-start.5 = (f32[4,64,1024]{2,1,0:T(8,128)}, f32[4,64,1024]{2,1,0:T(8,128)}, u32[]{:S(2)}, u32[]{:S(2)}) collective-permute-start(f32[4,64,1024]{2,1,0:T(8,128)} %copy.157), channel_id=1, source_target_pairs={{2,3},{6,7},{10,11},{14,15},{18,19},{22,23},{26,27},{30,31}} | collective-permute-start | bytes 3145736 | tf_op jit(solution)/shard_map/ppermute | solution.py:132
  498.7 65.5 %collective-permute-start.4 = (f32[4,64,1024]{2,1,0:T(8,128)S(1)}, f32[4,64,1024]{2,1,0:T(8,128)}, u32[]{:S(2)}, u32[]{:S(2)}) collective-permute-start(f32[4,64,1024]{2,1,0:T(8,128)S(1)} %copy.156), channel_id=1, source_target_pairs={{1,0},{5,4},{9,8},{13,12},{17,16},{21,20},{25,24},{29,28}} | collective-permute-start | bytes 3145736 | tf_op jit(solution)/shard_map/ppermute | solution.py:131
  504.2 73.5 %collective-permute-start.10 = (f32[4,64,1024]{2,1,0:T(8,128)}, f32[4,64,1024]{2,1,0:T(8,128)}, u32[]{:S(2)}, u32[]{:S(2)}) collective-permute-start(f32[4,64,1024]{2,1,0:T(8,128)} %copy.172), channel_id=1, source_target_pairs={{2,3},{6,7},{10,11},{14,15},{18,19},{22,23},{26,27},{30,31}} | collective-permute-start | bytes 3145736 | tf_op jit(solution)/shard_map/ppermute | solution.py:132
  522.5 59.9 %collective-permute-start.9 = (f32[4,64,1024]{2,1,0:T(8,128)}, f32[4,64,1024]{2,1,0:T(8,128)}, u32[]{:S(2)}, u32[]{:S(2)}) collective-permute-start(f32[4,64,1024]{2,1,0:T(8,128)} %copy.171), channel_id=1, source_target_pairs={{1,0},{5,4},{9,8},{13,12},{17,16},{21,20},{25,24},{29,28}} | collective-permute-start | bytes 3145736 | tf_op jit(solution)/shard_map/ppermute | solution.py:131
  537.7 56.8 %collective-permute-start.15 = (f32[4,64,1024]{2,1,0:T(8,128)}, f32[4,64,1024]{2,1,0:T(8,128)}, u32[]{:S(2)}, u32[]{:S(2)}) collective-permute-start(f32[4,64,1024]{2,1,0:T(8,128)} %copy.187), channel_id=1, source_target_pairs={{2,3},{6,7},{10,11},{14,15},{18,19},{22,23},{26,27},{30,31}} | collective-permute-start | bytes 3145736 | tf_op jit(solution)/shard_map/ppermute | solution.py:132
  559.9 37.4 %collective-permute-start.14 = (f32[4,64,1024]{2,1,0:T(8,128)}, f32[4,64,1024]{2,1,0:T(8,128)}, u32[]{:S(2)}, u32[]{:S(2)}) collective-permute-start(f32[4,64,1024]{2,1,0:T(8,128)} %copy.186), channel_id=1, source_target_pairs={{1,0},{5,4},{9,8},{13,12},{17,16},{21,20},{25,24},{29,28}} | collective-permute-start | bytes 3145736 | tf_op jit(solution)/shard_map/ppermute | solution.py:131
  564.3 35.8 %collective-permute-start.20 = (f32[4,64,1024]{2,1,0:T(8,128)}, f32[4,64,1024]{2,1,0:T(8,128)}, u32[]{:S(2)}, u32[]{:S(2)}) collective-permute-start(f32[4,64,1024]{2,1,0:T(8,128)} %copy.202), channel_id=1, source_target_pairs={{2,3},{6,7},{10,11},{14,15},{18,19},{22,23},{26,27},{30,31}} | collective-permute-start | bytes 3145736 | tf_op jit(solution)/shard_map/ppermute | solution.py:132
  569.2 4.5 copy-start.5
  569.2 4.7 copy-start.6
  577.8 34.4 %collective-permute-start.19 = (f32[4,64,1024]{2,1,0:T(8,128)}, f32[4,64,1024]{2,1,0:T(8,128)}, u32[]{:S(2)}, u32[]{:S(2)}) collective-permute-start(f32[4,64,1024]{2,1,0:T(8,128)} %copy.201), channel_id=1, source_target_pairs={{1,0},{5,4},{9,8},{13,12},{17,16},{21,20},{25,24},{29,28}} | collective-permute-start | bytes 3145736 | tf_op jit(solution)/shard_map/ppermute | solution.py:131
  585.2 4.5 copy-start.7
  602.8 4.5 copy-start.8
  615.1 4.6 copy-start.9
  619.7 3.9 copy-start.44
  619.7 3.9 copy-start.45
  (23 other events, 68.6 us)
Sparse Core Ops, SparseCore 0:
  133.5 61.7 all-reduce.2

commit v2 on v1

--- a/solution.py
+++ b/solution.py
@@ -4,6 +4,8 @@
 import jax.numpy as jnp
 from jax import lax
 from jax.sharding import PartitionSpec as P
+from jax.experimental import pallas as pl
+from jax.experimental.pallas import tpu as pltpu
 
 PP = 4
 NP = 4
@@ -93,34 +95,115 @@
     return lax.ppermute(values, "tm", [(0, 1), (groups - 1, groups - 2)])
 
 
+def whiten_kernel(rows_ref, forward_ref, mask_ref, out_ref):
+    spectrum = jnp.dot(rows_ref[...], forward_ref[...], preferred_element_type=jnp.float32)
+    energy = jnp.mean(spectrum * spectrum, axis=1, keepdims=True)
+    scaled = spectrum * lax.rsqrt(energy + 1e-06) * mask_ref[...]
+    out_ref[...] = scaled.astype(jnp.bfloat16).reshape(out_ref.shape)
+
+
+def whiten_segments(rows, mask, forward, chunks):
+    segments, channels, length = rows.shape
+    width = channels // chunks
+    return pl.pallas_call(
+        whiten_kernel,
+        grid=(segments,),
+        in_specs=[
+            pl.BlockSpec((None, channels, length), lambda m: (m, 0, 0)),
+            pl.BlockSpec((length, length), lambda m: (0, 0)),
+            pl.BlockSpec((None, channels, 1), lambda m: (m, 0, 0)),
+        ],
+        out_specs=pl.BlockSpec((chunks, None, width, length), lambda m: (0, m, 0, 0)),
+        out_shape=jax.ShapeDtypeStruct((chunks, segments, width, length), jnp.bfloat16),
+    )(rows, forward, mask)
+
+
+LANES = 128
+ROWS = 8
+
+
+def cross_kernel(own_ref, edge_ref, own_src_ref, edge_src_ref, out_ref):
+    segments = own_ref.shape[0]
+    sources = own_src_ref.shape[1]
+    bins = own_ref.shape[-1] // 2
+    for half in range(own_ref.shape[1] // ROWS):
+        rows = pl.ds(half * ROWS, ROWS)
+        for tile in range(bins // LANES):
+            re_lanes = pl.ds(tile * LANES, LANES)
+            im_lanes = pl.ds(bins + tile * LANES, LANES)
+
+            def step(m, acc, data_ref, src_ref):
+                wr = data_ref[m, rows, re_lanes].astype(jnp.float32)
+                wi = data_ref[m, rows, im_lanes].astype(jnp.float32)
+                out = []
+                for j in range(sources):
+                    sr = src_ref[m, j, :, re_lanes]
+                    si = src_ref[m, j, :, im_lanes]
+                    out.append(acc[2 * j] + (wr * sr + wi * si))
+                    out.append(acc[2 * j + 1] + (wi * sr - wr * si))
+                return tuple(out)
+
+            acc = tuple(jnp.zeros((ROWS, LANES), jnp.float32) for _ in range(2 * sources))
+            acc = lax.fori_loop(0, segments, lambda m, a: step(m, a, own_ref, own_src_ref), acc)
+            acc = lax.fori_loop(0, segments, lambda m, a: step(m, a, edge_ref, edge_src_ref), acc)
+            for j in range(sources):
+                out_ref[j, rows, re_lanes] = acc[2 * j]
+                out_ref[j, rows, im_lanes] = acc[2 * j + 1]
+
+
+def cross_chunk(own, edge, own_src, edge_src):
+    segments, width, length = own.shape
+    sources = own_src.shape[1]
+    step_rows = 2 * ROWS
+    return pl.pallas_call(
+        cross_kernel,
+        grid=(width // step_rows,),
+        in_specs=[
+            pl.BlockSpec((segments, step_rows, length), lambda i: (0, i, 0)),
+            pl.BlockSpec((segments, step_rows, length), lambda i: (0, i, 0)),
+            pl.BlockSpec((segments, sources, ROWS, length), lambda i: (0, 0, 0, 0)),
+            pl.BlockSpec((segments, sources, ROWS, length), lambda i: (0, 0, 0, 0)),
+        ],
+        out_specs=pl.BlockSpec((sources, step_rows, length), lambda i: (0, i, 0)),
+        out_shape=jax.ShapeDtypeStruct((sources, width, length), jnp.float32),
+    )(own, edge, own_src, edge_src)
+
+
 def on_line(traces, valid, panel_owner, panel_start):
     channels, windows_here, segments, length = traces.shape
     bins = length // 2
     groups = lax.axis_size("tm")
     place = lax.axis_index("tm")
+    chunks = 4
+    width = channels // chunks
+    seg_count = windows_here * segments
     forward = forward_table(length)
-    whitened = spectra_rows(
-        traces.reshape(channels * windows_here * segments, length),
-        valid.reshape(channels * windows_here * segments),
-        forward,
-    ).reshape(channels, windows_here * segments, 2 * bins)
+    rows = traces.reshape(channels, seg_count, length).transpose(1, 0, 2)
+    mask = valid.reshape(channels, seg_count).transpose(1, 0).astype(jnp.float32)[:, :, None]
+    whitened = whiten_segments(rows, mask, forward, chunks)
+    block_place = lax.axis_index("block")
     pieces = []
     for panel in range(NP):
-        pieces.append(fetch_panel(whitened, panel_owner[panel], panel_start[panel]))
-    sources = jnp.concatenate(pieces, axis=0)
-    source_count = sources.shape[0]
+        first = panel_start[panel]
+        chunk_of = first // width
+        candidate = lax.dynamic_slice_in_dim(
+            lax.dynamic_index_in_dim(whitened, chunk_of, 0, keepdims=False), first - chunk_of * width, PP, 1
+        )
+        pieces.append(jnp.where(block_place == panel_owner[panel], candidate, 0).astype(candidate.dtype))
+    sources = lax.psum(jnp.concatenate(pieces, axis=1), "block")
+    source_count = sources.shape[1]
     per_group = source_count // groups
     half = source_count // 2
     edge_sources = edge_first(sources, groups)
-    inverse = inverse_table(length, 1.0 / math.sqrt(bins * windows_here * segments * groups))
+    own_wide = jnp.broadcast_to(sources.astype(jnp.float32)[:, :, None, :], (seg_count, source_count, ROWS, length))
+    edge_wide = jnp.broadcast_to(edge_sources.astype(jnp.float32)[:, :, None, :], (seg_count, source_count, ROWS, length))
+    inverse = inverse_table(length, 1.0 / math.sqrt(bins * seg_count * groups))
     first_half = place < groups // 2
-    chunks = 4
-    width = channels // chunks
     outs = []
     for chunk in range(chunks):
-        own = whitened[chunk * width:(chunk + 1) * width]
+        own = whitened[chunk]
         edge_rows = edge_first(own, groups)
-        partial = correlate(sources, own) + correlate(edge_sources, edge_rows)
+        partial = cross_chunk(own, edge_rows, own_wide, edge_wide)
         low = partial[:half]
         high = partial[half:]
         to_right = lax.ppermute(high, "tm", [(1, 2)])

time: 645 us -> 445 us (0.69)
  the two profiles are of different devices: /device:TPU:16 before, /device:TPU:0 now
where the time goes in v2:
time: 445 us; the launch traced here: 444 us
  waiting for transfers between devices  154 us (35%)
  Pallas kernels  126 us (28%)
  starting transfers between devices  42.2 us (9%)
  local copies, waits for them, and re-layouts  41.9 us (9%)
  other arithmetic  35.4 us (8%)
  between operations  28.2 us (6%)
  matrix products  15.2 us (3%)
    pallas_call x4, Pallas kernels, cross_chunk(): pl.pallas_call(cross_kernel, grid=(width // step_rows,), in_specs=[pl.Blo...  111 us
    ppermute x4, waiting for transfers between devices, on_line(): back_left = lax.ppermute(lower, 'tm', [(1, 0)])  92.7 us
    psum x1, waiting for transfers between devices, on_line(): sources = lax.psum(jnp.concatenate(pieces, axis=1), 'block')  54.4 us
    ppermute x5, starting transfers between devices, edge_first(): return lax.ppermute(values, 'tm', [(0, 1), (groups - 1, groups - 2)])  19.3 us
    slice x4, local copies, waits for them, and re-layouts, on_line(): low = partial[:half]  17.3 us
    pallas_call x1, Pallas kernels, whiten_segments(): pl.pallas_call(whiten_kernel, grid=(segments,), in_specs=[pl.BlockSpec((N...  15.3 us
    dot_general x4, matrix products, on_line(): outs.append(jnp.dot(final, inverse, precision=lax.Precision.HIGHEST))  15.2 us
    select_n x4, other arithmetic, on_line(): total = jnp.where(first_half, low + to_left, high + to_right)  10.7 us
  transfers between devices with their start and end apart: 22, of which 6 were waited for; matrix products, arithmetic and copies ran while one was open for 14% of the time, Pallas kernels for 25%

profile of v2, /device:TPU:0, one launch (start us, length us, event | category | flops | bytes accessed | tf_op | source)
XLA Modules:
  0.0 443.5 jit_solution(8903846115445862656)
XLA Ops:
  6.5 8.5 %negate_convert_fusion = (bf16[1024,512]{1,0:T(8,128)(2,1)S(1)}, bf16[1024,512]{1,0:T(8,128)(2,1)S(1)}) fusion(), kind=kLoop, calls=%fused_computation.23 | loop fusion | flops 8912896 | bytes 2097152 | tf_op jit(solution)/shard_map/convert.1
  15.1 7.6 %copy.7 = bf16[256,2,6,1024]{3,0,2,1:T(8,128)(2,1)} copy(bf16[256,2,6,1024]{3,1,2,0:T(2,128)(2,1)} %param.4) | data formatting | bytes 12582912 | tf_op args[0]
  22.7 1.7 copy.9.mask_ref
  24.4 1.6 pad_maximum_fusion.1.forward_ref
  26.0 15.3 %shard_map.46 = bf16[4,12,64,1024]{3,2,1,0:T(8,128)(2,1)} custom-call(bf16[12,256,1024]{2,1,0:T(8,128)(2,1)} %bitcast.38, bf16[1024,1024]{1,0:T(8,128)(2,1)} %pad_maximum_fusion.1.forward_ref, f32[12,256,1]{2,1,0:T(8,128)} %copy.9.mask_ref), custom_call_target="tpu_custom_call" | custom-call | tf_op jit(solution)/shard_map/pallas_call | solution.py:108
  41.3 5.6 %slice_bitcast_fusion.3 = (bf16[12,64,1024]{2,1,0:T(8,128)(2,1)}, bf16[12,64,1024]{2,1,0:T(8,128)(2,1)S(1)}, bf16[12,64,1024]{2,1,0:T(8,128)(2,1)S(1)}, bf16[12,64,1024]{2,1,0:T(8,128)(2,1)}) fusion(bf16[4,12,64,1024]{3,2,1,0:T(8,128)(2,1)} %shard_map.46), kind=kLoop, calls=%fused_computation.36 | loop fusion | bytes 12582912 | tf_op jit(solution)/shard_map/squeeze | solution.py:204
  46.9 6.1 %collective-permute-start = (bf16[12,64,1024]{2,1,0:T(8,128)(2,1)}, bf16[12,64,1024]{2,1,0:T(8,128)(2,1)}, u32[]{:S(2)}, u32[]{:S(2)}) collective-permute-start(bf16[12,64,1024]{2,1,0:T(8,128)(2,1)} %get-tuple-element.5.own_ref), channel_id=1, source_target_pairs={{0,1},{3,2},{4,5},{7,6},{8,9},{11,10},{12,13},{15,14},{16,17},{19,... | collective-permute-start | bytes 4718600 | tf_op jit(solution)/shard_map/ppermute | solution.py:95
  53.0 2.4 collective-permute-start.6
  71.1 1.6 select_bitcast_fusion.3
  73.8 54.4 %all-reduce.2.cloned.1.call-done = bf16[12,16,1024]{2,1,0:T(8,128)(2,1)} async-done(((bf16[12,16,1024]{2,1,0:T(8,128)(2,1)}), bf16[12,16,1024]{2,1,0:T(8,128)(2,1)}) %all-reduce.2.cloned.1.call-update) | async-done | bytes 393232 | tf_op jit(solution)/shard_map/psum | solution.py:193
  128.2 3.4 collective-permute-start.1
  131.6 2.6 collective-permute-start.11
  134.1 7.3 %collective-permute-done.1 = bf16[12,16,1024]{2,1,0:T(8,128)(2,1)S(1)} collective-permute-done((bf16[12,16,1024]{2,1,0:T(8,128)(2,1)}, bf16[12,16,1024]{2,1,0:T(8,128)(2,1)S(1)}, u32[]{:S(2)}, u32[]{:S(2)}) %collective-permute-start.1) | collective-permute-done | bytes 393248 | tf_op jit(solution)/shard_map/ppermute | solution.py:95
  141.4 3.5 broadcast_in_dim.38.edge_src_ref
  144.9 3.5 broadcast_in_dim.37.own_src_ref
  148.4 27.7 %shard_map.47 = f32[16,64,1024]{2,1,0:T(8,128)} custom-call(bf16[12,64,1024]{2,1,0:T(8,128)(2,1)} %get-tuple-element.5.own_ref, bf16[12,64,1024]{2,1,0:T(8,128)(2,1)} %collective-permute-done.edge_ref, f32[12,16,8,1024]{3,2,1,0:T(8,128)} %broadcast_in_dim.37.own_src_ref, f32[12,16,8,1024]{3,2,1,0:T(8,128)} %broadcast_in_dim.38.edge_src_ref), custom_call_target="tpu_custom_call" | custom-call | tf_op jit(solution)/shard_map/pallas_call | solution.py:158
  176.1 4.8 %fusion.53 = (f32[8,64,1024]{2,1,0:T(8,128)}, f32[8,64,1024]{2,1,0:T(8,128)}) fusion(f32[16,64,1024]{2,1,0:T(8,128)} %shard_map.47), kind=kLoop, calls=%fused_computation.81 | loop fusion | bytes 8388608 | tf_op jit(solution)/shard_map/slice | solution.py:207
  180.9 2.0 collective-permute-start.2
  182.8 4.8 %collective-permute-start.16 = (bf16[12,64,1024]{2,1,0:T(8,128)(2,1)S(1)}, bf16[12,64,1024]{2,1,0:T(8,128)(2,1)}, u32[]{:S(2)}, u32[]{:S(2)}) collective-permute-start(bf16[12,64,1024]{2,1,0:T(8,128)(2,1)S(1)} %get-tuple-element.6.own_ref), channel_id=1, source_target_pairs={{0,1},{3,2},{4,5},{7,6},{8,9},{11,10},{12,13},{15,14},{16,17},{19,... | collective-permute-start | bytes 4718600 | tf_op jit(solution)/shard_map/ppermute | solution.py:95
  187.6 2.1 collective-permute-start.3
  189.7 27.8 %shard_map.48 = f32[16,64,1024]{2,1,0:T(8,128)} custom-call(bf16[12,64,1024]{2,1,0:T(8,128)(2,1)} %get-tuple-element.8.own_ref, bf16[12,64,1024]{2,1,0:T(8,128)(2,1)} %collective-permute-done.6.edge_ref, f32[12,16,8,1024]{3,2,1,0:T(8,128)} %broadcast_in_dim.37.own_src_ref, f32[12,16,8,1024]{3,2,1,0:T(8,128)} %broadcast_in_dim.38.edge_src_ref), custom_call_target="tpu_custom_call" | custom-call | tf_op jit(solution)/shard_map/pallas_call | solution.py:158
  217.5 4.8 %fusion.54 = (f32[8,64,1024]{2,1,0:T(8,128)}, f32[8,64,1024]{2,1,0:T(8,128)}) fusion(f32[16,64,1024]{2,1,0:T(8,128)} %shard_map.48), kind=kLoop, calls=%fused_computation.82 | loop fusion | bytes 8388608 | tf_op jit(solution)/shard_map/slice | solution.py:207
  222.3 2.0 collective-permute-start.7
  224.3 2.0 collective-permute-start.8
  226.3 27.8 %shard_map.49 = f32[16,64,1024]{2,1,0:T(8,128)} custom-call(bf16[12,64,1024]{2,1,0:T(8,128)(2,1)} %copy-done.6, bf16[12,64,1024]{2,1,0:T(8,128)(2,1)} %collective-permute-done.11.edge_ref, f32[12,16,8,1024]{3,2,1,0:T(8,128)} %broadcast_in_dim.37.own_src_ref, f32[12,16,8,1024]{3,2,1,0:T(8,128)} %broadcast_in_dim.38.edge_src_ref), custom_call_target="tpu_custom_call" | custom-call | tf_op jit(solution)/shard_map/pallas_call | solution.py:158
  254.1 4.9 %fusion.55 = (f32[8,64,1024]{2,1,0:T(8,128)}, f32[8,64,1024]{2,1,0:T(8,128)}) fusion(f32[16,64,1024]{2,1,0:T(8,128)} %shard_map.49), kind=kLoop, calls=%fused_computation.83 | loop fusion | bytes 8388608 | tf_op jit(solution)/shard_map/slice | solution.py:207
  259.0 2.0 collective-permute-start.12
  261.0 2.0 collective-permute-start.13
  263.0 9.2 %sine_multiply_fusion = (f32[512,1024]{1,0:T(8,128)S(1)}, f32[512,1024]{1,0:T(8,128)}) fusion(f32[512]{0:T(512)S(1)} %fusion.40, f32[512]{0:T(512)S(1)} %select_multiply_fusion), kind=kLoop, calls=%fused_computation.18 | loop fusion | flops 8388608 | bytes 4198400 | tf_op jit(solution)/shard_map/mul | solution.py:35
  272.2 27.7 %shard_map.50 = f32[16,64,1024]{2,1,0:T(8,128)} custom-call(bf16[12,64,1024]{2,1,0:T(8,128)(2,1)} %copy-done.5, bf16[12,64,1024]{2,1,0:T(8,128)(2,1)} %collective-permute-done.16.edge_ref, f32[12,16,8,1024]{3,2,1,0:T(8,128)} %broadcast_in_dim.37.own_src_ref, f32[12,16,8,1024]{3,2,1,0:T(8,128)} %broadcast_in_dim.38.edge_src_ref), custom_call_target="tpu_custom_call" | custom-call | tf_op jit(solution)/shard_map/pallas_call | solution.py:158
  299.9 2.9 fusion.56
  304.4 3.2 add_select_fusion.5
  307.9 1.6 collective-permute-start.4
  309.8 3.2 add_select_fusion.4
  315.2 3.2 add_select_fusion.3
  318.6 1.6 collective-permute-start.9
  320.2 1.3 collective-permute-start.14
  321.5 21.8 %collective-permute-done.4 = f32[4,64,1024]{2,1,0:T(8,128)S(1)} collective-permute-done((f32[4,64,1024]{2,1,0:T(8,128)S(1)}, f32[4,64,1024]{2,1,0:T(8,128)S(1)}, u32[]{:S(2)}, u32[]{:S(2)}) %collective-permute-start.4) | collective-permute-done | bytes 1048608 | tf_op jit(solution)/shard_map/ppermute | solution.py:214
  344.1 1.2 add_select_fusion.2
  345.5 1.4 collective-permute-start.19
  347.9 3.8 fusion.15
  351.7 37.2 %collective-permute-done.9 = f32[4,64,1024]{2,1,0:T(8,128)S(1)} collective-permute-done((f32[4,64,1024]{2,1,0:T(8,128)S(1)}, f32[4,64,1024]{2,1,0:T(8,128)S(1)}, u32[]{:S(2)}, u32[]{:S(2)}) %collective-permute-start.9) | collective-permute-done | bytes 1048608 | tf_op jit(solution)/shard_map/ppermute | solution.py:214
  388.9 3.8 fusion.14
  392.7 18.7 %collective-permute-done.14 = f32[4,64,1024]{2,1,0:T(8,128)S(1)} collective-permute-done((f32[4,64,1024]{2,1,0:T(8,128)S(1)}, f32[4,64,1024]{2,1,0:T(8,128)S(1)}, u32[]{:S(2)}, u32[]{:S(2)}) %collective-permute-start.14) | collective-permute-done | bytes 1048608 | tf_op jit(solution)/shard_map/ppermute | solution.py:214
  411.4 3.8 fusion.13
  415.2 15.0 %collective-permute-done.19 = f32[4,64,1024]{2,1,0:T(8,128)S(1)} collective-permute-done((f32[4,64,1024]{2,1,0:T(8,128)S(1)}, f32[4,64,1024]{2,1,0:T(8,128)S(1)}, u32[]{:S(2)}, u32[]{:S(2)}) %collective-permute-start.19) | collective-permute-done | bytes 1048608 | tf_op jit(solution)/shard_map/ppermute | solution.py:214
  430.2 3.8 fusion.12
  434.0 2.7 pad_maximum_fusion
  (58 shorter events, 8.8 us)
Async XLA Ops:
  6.5 121.6 %all-reduce.2.cloned.1.call-start = ((), (), s32[]{:S(2)}) async-start(), calls=%async_computation | async-start | bytes 786432 | tf_op jit(solution)/shard_map/psum | solution.py:193
  15.1 7.6 %copy-start.8 = (s32[256,2,6]{0,1,2:T(2,128)S(1)}, s32[256,2,6]{0,1,2:T(2,128)}, u32[]{:S(2)}) copy-start(s32[256,2,6]{0,1,2:T(2,128)} %param.5) | copy-start | bytes 36868
  41.3 14.2 %copy-start.9 = (s32[4]{0:T(128)S(1)}, s32[4]{0:T(128)}, u32[]{:S(2)}) copy-start(s32[4]{0:T(128)} %param.7) | copy-start | bytes 52
  41.3 26.8 %copy-start.10 = (s32[4]{0:T(128)S(1)}, s32[4]{0:T(128)}, u32[]{:S(2)}) copy-start(s32[4]{0:T(128)} %param.6) | copy-start | bytes 52
  46.9 98.0 %copy-start.6 = (bf16[12,64,1024]{2,1,0:T(8,128)(2,1)}, bf16[12,64,1024]{2,1,0:T(8,128)(2,1)S(1)}, u32[]{:S(2)}) copy-start(bf16[12,64,1024]{2,1,0:T(8,128)(2,1)S(1)} %get-tuple-element.7.own_ref) | copy-start | bytes 4718596
  46.9 135.9 %copy-start.5 = (bf16[12,64,1024]{2,1,0:T(8,128)(2,1)}, bf16[12,64,1024]{2,1,0:T(8,128)(2,1)S(1)}, u32[]{:S(2)}) copy-start(bf16[12,64,1024]{2,1,0:T(8,128)(2,1)S(1)} %get-tuple-element.6.own_ref) | copy-start | bytes 4718596
  46.9 94.4 %collective-permute-start = (bf16[12,64,1024]{2,1,0:T(8,128)(2,1)}, bf16[12,64,1024]{2,1,0:T(8,128)(2,1)}, u32[]{:S(2)}, u32[]{:S(2)}) collective-permute-start(bf16[12,64,1024]{2,1,0:T(8,128)(2,1)} %get-tuple-element.5.own_ref), channel_id=1, source_target_pairs={{0,1},{3,2},{4,5},{7,6},{8,9},{11,10},{12,13},{15,14},{16,17},{19,... | collective-permute-start | bytes 4718600 | tf_op jit(solution)/shard_map/ppermute | solution.py:95
  53.0 136.7 %collective-permute-start.6 = (bf16[12,64,1024]{2,1,0:T(8,128)(2,1)}, bf16[12,64,1024]{2,1,0:T(8,128)(2,1)}, u32[]{:S(2)}, u32[]{:S(2)}) collective-permute-start(bf16[12,64,1024]{2,1,0:T(8,128)(2,1)} %get-tuple-element.8.own_ref), channel_id=1, source_target_pairs={{0,1},{3,2},{4,5},{7,6},{8,9},{11,10},{12,13},{15,14},{16,17},{19,... | collective-permute-start | bytes 4718600 | tf_op jit(solution)/shard_map/ppermute | solution.py:95
  128.2 13.2 %collective-permute-start.1 = (bf16[12,16,1024]{2,1,0:T(8,128)(2,1)}, bf16[12,16,1024]{2,1,0:T(8,128)(2,1)S(1)}, u32[]{:S(2)}, u32[]{:S(2)}) collective-permute-start(bf16[12,16,1024]{2,1,0:T(8,128)(2,1)} %all-reduce.2.cloned.1.call-done), channel_id=1, source_target_pairs={{0,1},{3,2},{4,5},{7,6},{8,9},{11,10},{12,13},{15,14},{16,17},{19,... | collective-permute-start | bytes 1179656 | tf_op jit(solution)/shard_map/ppermute | solution.py:95
  131.5 13.3 %copy-start.7 = (bf16[12,16,1024]{2,1,0:T(8,128)(2,1)S(1)}, bf16[12,16,1024]{2,1,0:T(8,128)(2,1)}, u32[]{:S(2)}) copy-start(bf16[12,16,1024]{2,1,0:T(8,128)(2,1)} %all-reduce.2.cloned.1.call-done) | copy-start | bytes 1179652
  131.6 92.7 %collective-permute-start.11 = (bf16[12,64,1024]{2,1,0:T(8,128)(2,1)S(1)}, bf16[12,64,1024]{2,1,0:T(8,128)(2,1)}, u32[]{:S(2)}, u32[]{:S(2)}) collective-permute-start(bf16[12,64,1024]{2,1,0:T(8,128)(2,1)S(1)} %get-tuple-element.7.own_ref), channel_id=1, source_target_pairs={{0,1},{3,2},{4,5},{7,6},{8,9},{11,10},{12,13},{15,14},{16,17},{19,... | collective-permute-start | bytes 4718600 | tf_op jit(solution)/shard_map/ppermute | solution.py:95
  180.9 80.1 %collective-permute-start.2 = (f32[8,64,1024]{2,1,0:T(8,128)}, f32[8,64,1024]{2,1,0:T(8,128)}, u32[]{:S(2)}, u32[]{:S(2)}) collective-permute-start(f32[8,64,1024]{2,1,0:T(8,128)} %get-tuple-element.13), channel_id=1, source_target_pairs={{2,1},{6,5},{10,9},{14,13},{18,17},{22,21},{26,25},{30,29}} | collective-permute-start | bytes 6291464 | tf_op jit(solution)/shard_map/ppermute | solution.py:210
  182.8 76.1 %collective-permute-start.16 = (bf16[12,64,1024]{2,1,0:T(8,128)(2,1)S(1)}, bf16[12,64,1024]{2,1,0:T(8,128)(2,1)}, u32[]{:S(2)}, u32[]{:S(2)}) collective-permute-start(bf16[12,64,1024]{2,1,0:T(8,128)(2,1)S(1)} %get-tuple-element.6.own_ref), channel_id=1, source_target_pairs={{0,1},{3,2},{4,5},{7,6},{8,9},{11,10},{12,13},{15,14},{16,17},{19,... | collective-permute-start | bytes 4718600 | tf_op jit(solution)/shard_map/ppermute | solution.py:95
  187.6 115.2 %collective-permute-start.3 = (f32[8,64,1024]{2,1,0:T(8,128)}, f32[8,64,1024]{2,1,0:T(8,128)}, u32[]{:S(2)}, u32[]{:S(2)}) collective-permute-start(f32[8,64,1024]{2,1,0:T(8,128)} %get-tuple-element.14), channel_id=1, source_target_pairs={{1,2},{5,6},{9,10},{13,14},{17,18},{21,22},{25,26},{29,30}} | collective-permute-start | bytes 6291464 | tf_op jit(solution)/shard_map/ppermute | solution.py:209
  222.3 81.4 %collective-permute-start.7 = (f32[8,64,1024]{2,1,0:T(8,128)}, f32[8,64,1024]{2,1,0:T(8,128)}, u32[]{:S(2)}, u32[]{:S(2)}) collective-permute-start(f32[8,64,1024]{2,1,0:T(8,128)} %get-tuple-element.15), channel_id=1, source_target_pairs={{2,1},{6,5},{10,9},{14,13},{18,17},{22,21},{26,25},{30,29}} | collective-permute-start | bytes 6291464 | tf_op jit(solution)/shard_map/ppermute | solution.py:210
  224.3 83.6 %collective-permute-start.8 = (f32[8,64,1024]{2,1,0:T(8,128)}, f32[8,64,1024]{2,1,0:T(8,128)}, u32[]{:S(2)}, u32[]{:S(2)}) collective-permute-start(f32[8,64,1024]{2,1,0:T(8,128)} %get-tuple-element.16), channel_id=1, source_target_pairs={{1,2},{5,6},{9,10},{13,14},{17,18},{21,22},{25,26},{29,30}} | collective-permute-start | bytes 6291464 | tf_op jit(solution)/shard_map/ppermute | solution.py:209
  259.0 54.3 %collective-permute-start.12 = (f32[8,64,1024]{2,1,0:T(8,128)}, f32[8,64,1024]{2,1,0:T(8,128)}, u32[]{:S(2)}, u32[]{:S(2)}) collective-permute-start(f32[8,64,1024]{2,1,0:T(8,128)} %get-tuple-element.17), channel_id=1, source_target_pairs={{2,1},{6,5},{10,9},{14,13},{18,17},{22,21},{26,25},{30,29}} | collective-permute-start | bytes 6291464 | tf_op jit(solution)/shard_map/ppermute | solution.py:210
  261.0 53.2 %collective-permute-start.13 = (f32[8,64,1024]{2,1,0:T(8,128)}, f32[8,64,1024]{2,1,0:T(8,128)}, u32[]{:S(2)}, u32[]{:S(2)}) collective-permute-start(f32[8,64,1024]{2,1,0:T(8,128)} %get-tuple-element.18), channel_id=1, source_target_pairs={{1,2},{5,6},{9,10},{13,14},{17,18},{21,22},{25,26},{29,30}} | collective-permute-start | bytes 6291464 | tf_op jit(solution)/shard_map/ppermute | solution.py:209
  299.9 4.5 %copy-start.1 = (f32[16,64,1024]{2,1,0:T(8,128)S(1)}, f32[16,64,1024]{2,1,0:T(8,128)}, u32[]{:S(2)}) copy-start(f32[16,64,1024]{2,1,0:T(8,128)} %shard_map.47) | copy-start | bytes 12582916
  302.8 15.8 %collective-permute-start.17 = (f32[8,64,1024]{2,1,0:T(8,128)S(1)}, f32[8,64,1024]{2,1,0:T(8,128)S(1)}, u32[]{:S(2)}, u32[]{:S(2)}) collective-permute-start(f32[8,64,1024]{2,1,0:T(8,128)S(1)} %get-tuple-element.19), channel_id=1, source_target_pairs={{2,1},{6,5},{10,9},{14,13},{18,17},{22,21},{26,25},{30,29}} | collective-permute-start | bytes 6291464 | tf_op jit(solution)/shard_map/ppermute | solution.py:210
  303.6 16.6 %collective-permute-start.18 = (f32[8,64,1024]{2,1,0:T(8,128)S(1)}, f32[8,64,1024]{2,1,0:T(8,128)S(1)}, u32[]{:S(2)}, u32[]{:S(2)}) collective-permute-start(f32[8,64,1024]{2,1,0:T(8,128)S(1)} %get-tuple-element.20), channel_id=1, source_target_pairs={{1,2},{5,6},{9,10},{13,14},{17,18},{21,22},{25,26},{29,30}} | collective-permute-start | bytes 6291464 | tf_op jit(solution)/shard_map/ppermute | solution.py:209
  307.6 2.2 copy-start.2
  307.9 35.4 %collective-permute-start.4 = (f32[4,64,1024]{2,1,0:T(8,128)S(1)}, f32[4,64,1024]{2,1,0:T(8,128)S(1)}, u32[]{:S(2)}, u32[]{:S(2)}) collective-permute-start(f32[4,64,1024]{2,1,0:T(8,128)S(1)} %get-tuple-element.22), channel_id=1, source_target_pairs={{1,0},{5,4},{9,8},{13,12},{17,16},{21,20},{25,24},{29,28}} | collective-permute-start | bytes 3145736 | tf_op jit(solution)/shard_map/ppermute | solution.py:214
  313.0 2.2 copy-start.4
  313.3 32.2 %collective-permute-start.5 = (f32[4,64,1024]{2,1,0:T(8,128)S(1)}, f32[4,64,1024]{2,1,0:T(8,128)S(1)}, u32[]{:S(2)}, u32[]{:S(2)}) collective-permute-start(f32[4,64,1024]{2,1,0:T(8,128)S(1)} %get-tuple-element.21), channel_id=1, source_target_pairs={{2,3},{6,7},{10,11},{14,15},{18,19},{22,23},{26,27},{30,31}} | collective-permute-start | bytes 3145736 | tf_op jit(solution)/shard_map/ppermute | solution.py:215
  314.1 32.8 %collective-permute-start.10 = (f32[4,64,1024]{2,1,0:T(8,128)S(1)}, f32[4,64,1024]{2,1,0:T(8,128)S(1)}, u32[]{:S(2)}, u32[]{:S(2)}) collective-permute-start(f32[4,64,1024]{2,1,0:T(8,128)S(1)} %get-tuple-element.23), channel_id=1, source_target_pairs={{2,3},{6,7},{10,11},{14,15},{18,19},{22,23},{26,27},{30,31}} | collective-permute-start | bytes 3145736 | tf_op jit(solution)/shard_map/ppermute | solution.py:215
  318.4 25.7 %copy-start.3 = (f32[16,64,1024]{2,1,0:T(8,128)S(1)}, f32[16,64,1024]{2,1,0:T(8,128)}, u32[]{:S(2)}) copy-start(f32[16,64,1024]{2,1,0:T(8,128)} %shard_map.50) | copy-start | bytes 12582916
  318.6 70.3 %collective-permute-start.9 = (f32[4,64,1024]{2,1,0:T(8,128)S(1)}, f32[4,64,1024]{2,1,0:T(8,128)S(1)}, u32[]{:S(2)}, u32[]{:S(2)}) collective-permute-start(f32[4,64,1024]{2,1,0:T(8,128)S(1)} %get-tuple-element.24), channel_id=1, source_target_pairs={{1,0},{5,4},{9,8},{13,12},{17,16},{21,20},{25,24},{29,28}} | collective-permute-start | bytes 3145736 | tf_op jit(solution)/shard_map/ppermute | solution.py:214
  320.2 91.2 %collective-permute-start.14 = (f32[4,64,1024]{2,1,0:T(8,128)S(1)}, f32[4,64,1024]{2,1,0:T(8,128)S(1)}, u32[]{:S(2)}, u32[]{:S(2)}) collective-permute-start(f32[4,64,1024]{2,1,0:T(8,128)S(1)} %get-tuple-element.26), channel_id=1, source_target_pairs={{1,0},{5,4},{9,8},{13,12},{17,16},{21,20},{25,24},{29,28}} | collective-permute-start | bytes 3145736 | tf_op jit(solution)/shard_map/ppermute | solution.py:214
  343.3 68.1 %collective-permute-start.15 = (f32[4,64,1024]{2,1,0:T(8,128)S(1)}, f32[4,64,1024]{2,1,0:T(8,128)S(1)}, u32[]{:S(2)}, u32[]{:S(2)}) collective-permute-start(f32[4,64,1024]{2,1,0:T(8,128)S(1)} %get-tuple-element.25), channel_id=1, source_target_pairs={{2,3},{6,7},{10,11},{14,15},{18,19},{22,23},{26,27},{30,31}} | collective-permute-start | bytes 3145736 | tf_op jit(solution)/shard_map/ppermute | solution.py:215
  345.2 2.7 copy-start
  345.5 84.7 %collective-permute-start.19 = (f32[4,64,1024]{2,1,0:T(8,128)S(1)}, f32[4,64,1024]{2,1,0:T(8,128)S(1)}, u32[]{:S(2)}, u32[]{:S(2)}) collective-permute-start(f32[4,64,1024]{2,1,0:T(8,128)S(1)} %get-tuple-element.28), channel_id=1, source_target_pairs={{1,0},{5,4},{9,8},{13,12},{17,16},{21,20},{25,24},{29,28}} | collective-permute-start | bytes 3145736 | tf_op jit(solution)/shard_map/ppermute | solution.py:214
  346.9 83.3 %collective-permute-start.20 = (f32[4,64,1024]{2,1,0:T(8,128)S(1)}, f32[4,64,1024]{2,1,0:T(8,128)S(1)}, u32[]{:S(2)}, u32[]{:S(2)}) collective-permute-start(f32[4,64,1024]{2,1,0:T(8,128)S(1)} %get-tuple-element.27), channel_id=1, source_target_pairs={{2,3},{6,7},{10,11},{14,15},{18,19},{22,23},{26,27},{30,31}} | collective-permute-start | bytes 3145736 | tf_op jit(solution)/shard_map/ppermute | solution.py:215
Sparse Core Ops, SparseCore 0:
  73.9 54.2 all-reduce.1
